TPU v7x, 32 devices: a whole 2x2x4 slice. The times are simulated.
32 devices in a mesh: dp: 4 (over x, core), pipe: 2 (over y), tensor: 4 (over z).
Axes of the slice: x: 2, y: 2, z: 4, core: 2. Of those that a mesh axis runs over, the one named last changes fastest.
Arguments:
- layer_input: bfloat16 [4, 2, 512, 8192], P('dp', 'pipe', None, 'tensor'), may hold values from -40 to 40
- output_grad: bfloat16 [4, 2, 512, 8192], P('dp', 'pipe', None, 'tensor'), may hold values from -6 to 6
- kv_grad: bfloat16 [4, 2, 512, 2048], P('dp', 'pipe', None, 'tensor'), may hold values from -6 to 6
- norm_gain: bfloat16 [2, 8192], P('pipe', 'tensor'), may hold values from 0.5 to 1.5
- kv_weight: bfloat16 [2, 8192, 2048], P('pipe', 'tensor'), may hold values from -0.0625 to 0.0625
Outputs:
- upstream_grad: bfloat16 [4, 2, 512, 8192], P('dp', 'pipe', None, 'tensor')
- kv_weight_grad: bfloat16 [2, 8192, 2048], P('pipe', 'tensor', 'dp')
- gain_grad: float32 [2, 8192], P('pipe', 'tensor')
All inputs are finite; a program needn't handle non-finite values.
Results may differ from a plain program's by a relative error of at most 0.009.
Values may be sent and summed in bfloat16 or wider, within the bound.
No kernel may reach another device: no remote copies, remote signals or barrier semaphores. Data moves between devices by JAX's collectives and lax.ppermute only.
A program may use at most 128 MiB of HBM per device.

v0:
```python
import jax
import jax.numpy as jnp
from jax import lax
from jax.sharding import PartitionSpec as P

D = 8192


def from_behind(block, axis, distance):
    devices = range(lax.axis_size(axis))
    route = [(i - distance, i) for i in devices if i - distance in devices]
    return lax.ppermute(block, axis, route)


def on_device(layer_input, output_grad, kv_grad, norm_gain, kv_weight):
    rows = layer_input[0, 0]
    grad_out = output_grad[0, 0]
    grad_kv = kv_grad[0, 0]
    gain_f = norm_gain[0].astype(jnp.float32)
    weight = kv_weight[0]
    values = rows.astype(jnp.float32)
    local_squares = jnp.sum(values * values, axis=1, keepdims=True)
    total_squares = lax.psum(local_squares, "tensor")
    rstd = lax.rsqrt(total_squares / D + 1e-05)
    normed = values * rstd
    hidden = (normed * gain_f).astype(jnp.bfloat16)
    piece = lax.all_gather(grad_kv, "tensor", axis=1, tiled=True)
    row_total = lax.dot_general(
        piece, weight, (((1,), (1,)), ((), ())), preferred_element_type=jnp.float32
    )
    term = lax.dot_general(
        hidden, piece, (((0,), (0,)), ((), ())), preferred_element_type=jnp.float32
    )
    weight_total = term
    wgrad = weight_total
    scaled = gain_f * row_total
    local_dot = jnp.sum(scaled * normed, axis=1, keepdims=True)
    mean_term = lax.psum(local_dot, "tensor") / D
    input_grad = (grad_out.astype(jnp.float32) + rstd * (scaled - normed * mean_term)).astype(
        jnp.bfloat16
    )
    upstream = from_behind(input_grad, "pipe", -1)
    gain_part = jnp.sum(row_total * normed, axis=0)
    gain_total = lax.psum(gain_part, "dp")
    weight_total = lax.psum_scatter(
        wgrad.astype(jnp.bfloat16), "dp", scatter_dimension=1, tiled=True
    )
    return (upstream[None, None], weight_total[None], gain_total[None])


def solution(mesh):
    in_specs = (
        P("dp", "pipe", None, "tensor"),
        P("dp", "pipe", None, "tensor"),
        P("dp", "pipe", None, "tensor"),
        P("pipe", "tensor"),
        P("pipe", "tensor", None),
    )
    out_specs = (P("dp", "pipe", None, "tensor"), P("pipe", "tensor", "dp"), P("pipe", "tensor"))
    return jax.shard_map(
        on_device, mesh=mesh, in_specs=in_specs, out_specs=out_specs, check_vma=False
    )
```

profile of v0, /device:TPU:0, one launch (start us, length us, event | category | flops | bytes accessed | tf_op | source)
XLA Modules:
  0.0 152.9 jit_solution(5806783644709270451)
XLA Ops:
  7.2 0.0 all-gather.3.cloned.1.call-start
  7.2 0.7 all-gather.3.cloned.1.call-update
  7.9 0.0 reduce-scatter.2.cloned.1.call-start
  7.9 0.7 mul.69
  8.7 2.1 %fusion.13 = f32[512]{0:T(512)S(1)} fusion(bf16[1,1,512,2048]{3,2,1,0:T(8,128)(2,1)} %param.5), kind=kLoop, calls=%fused_computation.16 | loop fusion | flops 3145216 | bytes 2099200 | tf_op jit(solution)/shard_map/reduce_sum | solution.py:22
  10.7 13.7 %psum.21 = f32[512,1]{0,1:T(1,128)S(1)} all-reduce(f32[512,1]{0,1:T(1,128)S(1)} %bitcast.37), channel_id=1, replica_groups=mesh['dp'=4,'pipe'=2,'tensor'=4] {'tensor'}, use_global_device_ids=true, to_apply=%region_1.0 | all-reduce | flops 512 | bytes 4096 | tf_op jit(solution)/shard_map/psum | solution.py:23
  24.4 33.9 %all-gather.3.cloned.1.call-done = bf16[1,1,512,2048]{3,2,1,0:T(8,128)(2,1)} async-done(((bf16[1,1,512,512]{3,2,1,0:T(8,128)(2,1)}), bf16[1,1,512,2048]{3,2,1,0:T(8,128)(2,1)}) %all-gather.3.cloned.1.call-update) | async-done | bytes 2097168 | tf_op jit(solution)/shard_map/all_gather | solution.py:27
  58.3 10.1 %convolution_convert_fusion = bf16[2048,2048]{1,0:T(8,128)(2,1)} fusion(bf16[1,1,512,2048]{3,2,1,0:T(8,128)(2,1)} %param.5, bf16[1,1,512,2048]{3,2,1,0:T(8,128)(2,1)} %all-gather.3.cloned.1.call-done, f32[2048]{0:T(1024)S(1)} %bitcast.34, f32[512]{0:T(512)S(1)} %bitcast.39), kind=kOutput, calls=%fused_computation.2 | convolution fusion | flops 4303355904 | bytes 12593152 | tf_op jit(solution)/shard_map/dot_general | solution.py:31
  68.4 0.0 copy-start
  68.4 0.0 reduce-scatter.2.cloned.1.call-update
  68.4 1.6 %copy-done = bf16[1,1,512,2048]{3,2,1,0:T(8,128)(2,1)S(1)} copy-done((bf16[1,1,512,2048]{3,2,1,0:T(8,128)(2,1)S(1)}, bf16[1,1,512,2048]{3,2,1,0:T(8,128)(2,1)}, u32[]{:S(2)}) %copy-start) | copy-done | bytes 2097176
  70.0 11.8 %fusion.12 = (f32[2048]{0:T(1024)S(1)}, f32[512]{0:T(512)S(1)}, f32[512,2048]{1,0:T(8,128)}) fusion(bf16[1,1,512,2048]{3,2,1,0:T(8,128)(2,1)S(1)} %copy-done, f32[512]{0:T(512)S(1)} %bitcast.40, f32[2048]{0:T(1024)S(1)} %bitcast.35, bf16[1,2048,2048]{2,1,0:T(8,128)(2,1)} %param.9, bf16[1,1,512,2048]{3,2,1,0:T(8,128)(2,1)} %all-gather.3.cloned.1.call-done), kind=kOutput, calls=%fused_computation.15 | convolution fusion | flops 4302304768 | bytes 16797696 | tf_op jit(solution)/shard_map/dot_general | solution.py:28
  81.8 9.0 %psum.22 = f32[512,1]{0,1:T(1,128)S(1)} all-reduce(f32[512,1]{0,1:T(1,128)S(1)} %bitcast.43), channel_id=1, replica_groups=mesh['dp'=4,'pipe'=2,'tensor'=4] {'tensor'}, use_global_device_ids=true, to_apply=%region_3.0 | all-reduce | flops 512 | bytes 4096 | tf_op jit(solution)/shard_map/psum | solution.py:38
  90.8 5.7 %fusion.10 = bf16[512,2048]{1,0:T(8,128)(2,1)} fusion(f32[512,2048]{1,0:T(8,128)} %get-tuple-element.5, bf16[1,1,512,2048]{3,2,1,0:T(8,128)(2,1)} %param.6, bf16[1,1,512,2048]{3,2,1,0:T(8,128)(2,1)S(1)} %copy-done, f32[512]{0:T(512)S(1)} %bitcast.42, f32[2048]{0:T(1024)S(1)} %bitcast.36, f32[512]{0:T(512)S(1)} %bitcast.41), kind=kLoop, calls=%fused_computation.13 | loop fusion | flops 9437184 | bytes 10498048 | tf_op jit(solution)/shard_map/convert_element_type | solution.py:39
  96.5 1.3 collective-permute-start
  97.8 7.0 %psum.23 = f32[1,2048]{1,0:T(1,128)} all-reduce(f32[1,2048]{1,0:T(1,128)S(1)} %bitcast.38), channel_id=1, replica_groups=mesh['dp'=4,'pipe'=2,'tensor'=4] {'dp'}, use_global_device_ids=true, to_apply=%region_6.0 | all-reduce | flops 2048 | bytes 16384 | tf_op jit(solution)/shard_map/psum | solution.py:44
  104.8 39.9 %collective-permute-done = bf16[512,2048]{1,0:T(8,128)(2,1)S(1)} collective-permute-done((bf16[512,2048]{1,0:T(8,128)(2,1)}, bf16[512,2048]{1,0:T(8,128)(2,1)S(1)}, u32[]{:S(2)}, u32[]{:S(2)}) %collective-permute-start) | collective-permute-done | bytes 2097184 | tf_op jit(solution)/shard_map/ppermute | solution.py:12
  144.7 0.0 reduce-scatter.2.cloned.1.call-done
  144.7 1.3 copy.9
  (2 shorter events, 0.0 us)
Async XLA Ops:
  7.2 51.1 %all-gather.3.cloned.1.call-start = ((), (), s32[]{:S(2)}) async-start(), calls=%async_computation.2 | async-start | bytes 2621440 | tf_op jit(solution)/shard_map/all_gather | solution.py:27
  7.9 136.8 %reduce-scatter.2.cloned.1.call-start = ((), (), s32[]{:S(2)}) async-start(), calls=%async_computation.1 | async-start | bytes 10485760 | tf_op jit(solution)/shard_map/reduce_scatter | solution.py:45
  68.4 1.6 %copy-start = (bf16[1,1,512,2048]{3,2,1,0:T(8,128)(2,1)S(1)}, bf16[1,1,512,2048]{3,2,1,0:T(8,128)(2,1)}, u32[]{:S(2)}) copy-start(bf16[1,1,512,2048]{3,2,1,0:T(8,128)(2,1)} %param.5) | copy-start | bytes 6291460
  96.5 48.2 %collective-permute-start = (bf16[512,2048]{1,0:T(8,128)(2,1)}, bf16[512,2048]{1,0:T(8,128)(2,1)S(1)}, u32[]{:S(2)}, u32[]{:S(2)}) collective-permute-start(bf16[512,2048]{1,0:T(8,128)(2,1)} %fusion.10), channel_id=1, source_target_pairs={{4,0},{5,1},{6,2},{7,3},{12,8},{13,9},{14,10},{15,11},{20,16},{21,... | collective-permute-start | bytes 6291464 | tf_op jit(solution)/shard_map/ppermute | solution.py:12
Sparse Core Ops, SparseCore 0:
  9.6 48.6 all-gather.2
  68.5 70.6 reduce-scatter.1
where the time goes:
time: 153 us
  waiting for transfers between devices  74.5 us (49%)
  blocking collectives  29.6 us (19%)
  matrix products  21.9 us (14%)
  between operations  14.1 us (9%)
  other arithmetic  8.53 us (6%)
  local copies, waits for them, and re-layouts  2.89 us (2%)
    ppermute x1, waiting for transfers between devices, from_behind(): return lax.ppermute(block, axis, route)  39.9 us
    all_gather x1, waiting for transfers between devices, on_device(): piece = lax.all_gather(grad_kv, 'tensor', axis=1, tiled=True)  33.9 us
    psum x1, blocking collectives, on_device(): total_squares = lax.psum(local_squares, 'tensor')  13.7 us
    dot_general x1, matrix products, on_device(): lax.dot_general(piece, weight, (((1,), (1,)), ((), ())), preferred_elemen...  11.8 us
    dot_general x1, matrix products, on_device(): lax.dot_general(hidden, piece, (((0,), (0,)), ((), ())), preferred_elemen...  10.1 us
    psum x1, blocking collectives, on_device(): mean_term = lax.psum(local_dot, 'tensor') / D  8.96 us
    psum x1, blocking collectives, on_device(): gain_total = lax.psum(gain_part, 'dp')  7.03 us
    convert_element_type x1, other arithmetic, on_device(): (grad_out.astype(jnp.float32) + rstd * (scaled - normed * mean_term)).ast...  5.73 us
  transfers between devices with their start and end apart: 3, of which 2 were waited for; matrix products, arithmetic and copies ran while one was open for 13% of the time, Pallas kernels for 0%

commit v1 on v0

--- a/solution.py
+++ b/solution.py
@@ -20,7 +20,7 @@
     weight = kv_weight[0]
     values = rows.astype(jnp.float32)
     local_squares = jnp.sum(values * values, axis=1, keepdims=True)
-    total_squares = lax.psum(local_squares, "tensor")
+    total_squares = jnp.sum(lax.all_gather(local_squares, "tensor"), axis=0)
     rstd = lax.rsqrt(total_squares / D + 1e-05)
     normed = values * rstd
     hidden = (normed * gain_f).astype(jnp.bfloat16)

time: 153 us -> 153 us (level)
    psum x1 -> x0, blocking collectives: 13.7 us -> none  [on_device(): total_squares = lax.psum(local_squares, 'tensor')]
    all_gather x0 -> x1, blocking collectives: none -> 13.6 us  [on_device(): total_squares = jnp.sum(lax.all_gather(local_squares, 'tensor'), axis=0)]
where the time goes in v1:
time: 153 us
  waiting for transfers between devices  74.2 us (48%)
  blocking collectives  29.6 us (19%)
  matrix products  22 us (14%)
  between operations  14.1 us (9%)
  other arithmetic  8.68 us (6%)
  local copies, waits for them, and re-layouts  2.89 us (2%)
    ppermute x1, waiting for transfers between devices, from_behind(): return lax.ppermute(block, axis, route)  39.7 us
    all_gather x1, waiting for transfers between devices, on_device(): piece = lax.all_gather(grad_kv, 'tensor', axis=1, tiled=True)  33.8 us
    all_gather x1, blocking collectives, on_device(): total_squares = jnp.sum(lax.all_gather(local_squares, 'tensor'), axis=0)  13.6 us
    dot_general x1, matrix products, on_device(): lax.dot_general(piece, weight, (((1,), (1,)), ((), ())), preferred_elemen...  11.8 us
    dot_general x1, matrix products, on_device(): lax.dot_general(hidden, piece, (((0,), (0,)), ((), ())), preferred_elemen...  10.1 us
    psum x1, blocking collectives, on_device(): mean_term = lax.psum(local_dot, 'tensor') / D  8.89 us
    psum x1, blocking collectives, on_device(): gain_total = lax.psum(gain_part, 'dp')  7.03 us
    convert_element_type x1, other arithmetic, on_device(): (grad_out.astype(jnp.float32) + rstd * (scaled - normed * mean_term)).ast...  5.86 us
  transfers between devices with their start and end apart: 3, of which 2 were waited for; matrix products, arithmetic and copies ran while one was open for 13% of the time, Pallas kernels for 0%

profile of v1, /device:TPU:0, one launch (start us, length us, event | category | flops | bytes accessed | tf_op | source)
XLA Modules:
  0.0 152.7 jit_solution(17640072642552504765)
XLA Ops:
  7.2 0.0 all-gather.5.cloned.1.call-start
  7.2 0.7 all-gather.5.cloned.1.call-update
  7.9 0.0 reduce-scatter.2.cloned.1.call-start
  7.9 0.7 mul.66
  8.7 2.1 %fusion.13 = f32[512]{0:T(512)S(1)} fusion(bf16[1,1,512,2048]{3,2,1,0:T(8,128)(2,1)} %param.5), kind=kLoop, calls=%fused_computation.16 | loop fusion | flops 3145216 | bytes 2099200 | tf_op jit(solution)/shard_map/reduce_sum | solution.py:22
  10.7 13.6 %all-gather.2 = f32[4,1,512]{2,1,0:T(1,128)S(1)} all-gather(f32[1,1,512]{2,1,0:T(1,128)S(1)} %bitcast.36), channel_id=2, replica_groups=mesh['dp'=4,'pipe'=2,'tensor'=4] {'tensor'}, dimensions={0}, use_global_device_ids=true | all-gather | bytes 10240 | tf_op jit(solution)/shard_map/all_gather | solution.py:23
  24.4 33.8 %all-gather.5.cloned.1.call-done = bf16[1,1,512,2048]{3,2,1,0:T(8,128)(2,1)} async-done(((bf16[1,1,512,512]{3,2,1,0:T(8,128)(2,1)}), bf16[1,1,512,2048]{3,2,1,0:T(8,128)(2,1)}) %all-gather.5.cloned.1.call-update) | async-done | bytes 2097168 | tf_op jit(solution)/shard_map/all_gather | solution.py:27
  58.3 10.1 %convolution_convert_fusion = bf16[2048,2048]{1,0:T(8,128)(2,1)} fusion(bf16[1,1,512,2048]{3,2,1,0:T(8,128)(2,1)} %param.5, bf16[1,1,512,2048]{3,2,1,0:T(8,128)(2,1)} %all-gather.5.cloned.1.call-done, f32[2048]{0:T(1024)S(1)} %bitcast.33, f32[512]{0:T(512)S(1)} %add_rsqrt_fusion), kind=kOutput, calls=%fused_computation.2 | convolution fusion | flops 4303355904 | bytes 12593152 | tf_op jit(solution)/shard_map/dot_general | solution.py:31
  68.4 0.0 copy-start
  68.4 0.0 reduce-scatter.2.cloned.1.call-update
  68.4 1.6 %copy-done = bf16[1,1,512,2048]{3,2,1,0:T(8,128)(2,1)S(1)} copy-done((bf16[1,1,512,2048]{3,2,1,0:T(8,128)(2,1)S(1)}, bf16[1,1,512,2048]{3,2,1,0:T(8,128)(2,1)}, u32[]{:S(2)}) %copy-start) | copy-done | bytes 2097176
  70.0 11.8 %fusion.12 = (f32[2048]{0:T(1024)S(1)}, f32[512]{0:T(512)S(1)}, f32[512,2048]{1,0:T(8,128)}) fusion(bf16[1,1,512,2048]{3,2,1,0:T(8,128)(2,1)S(1)} %copy-done, f32[512]{0:T(512)S(1)} %add_rsqrt_fusion, f32[2048]{0:T(1024)S(1)} %bitcast.34, bf16[1,2048,2048]{2,1,0:T(8,128)(2,1)} %param.9, bf16[1,1,512,2048]{3,2,1,0:T(8,128)(2,1)} %all-gather.5.cloned.1.call-done), kind=kOutput, calls=%fused_computation.15 | convolution fusion | flops 4302304768 | bytes 16797696 | tf_op jit(solution)/shard_map/dot_general | solution.py:28
  81.8 8.9 %psum.14 = f32[512,1]{0,1:T(1,128)S(1)} all-reduce(f32[512,1]{0,1:T(1,128)S(1)} %bitcast.39), channel_id=1, replica_groups=mesh['dp'=4,'pipe'=2,'tensor'=4] {'tensor'}, use_global_device_ids=true, to_apply=%region_3.0 | all-reduce | flops 512 | bytes 4096 | tf_op jit(solution)/shard_map/psum | solution.py:38
  90.7 5.9 %fusion.10 = bf16[512,2048]{1,0:T(8,128)(2,1)} fusion(f32[512,2048]{1,0:T(8,128)} %get-tuple-element.5, bf16[1,1,512,2048]{3,2,1,0:T(8,128)(2,1)} %param.6, bf16[1,1,512,2048]{3,2,1,0:T(8,128)(2,1)S(1)} %copy-done, f32[512]{0:T(512)S(1)} %bitcast.38, f32[2048]{0:T(1024)S(1)} %bitcast.35, f32[512]{0:T(512)S(1)} %add_rsqrt_fusion), kind=kLoop, calls=%fused_computation.13 | loop fusion | flops 9437184 | bytes 10498048 | tf_op jit(solution)/shard_map/convert_element_type | solution.py:39
  96.6 1.3 collective-permute-start
  97.9 7.0 %psum.15 = f32[1,2048]{1,0:T(1,128)} all-reduce(f32[1,2048]{1,0:T(1,128)S(1)} %bitcast.37), channel_id=1, replica_groups=mesh['dp'=4,'pipe'=2,'tensor'=4] {'dp'}, use_global_device_ids=true, to_apply=%region_6.0 | all-reduce | flops 2048 | bytes 16384 | tf_op jit(solution)/shard_map/psum | solution.py:44
  104.9 39.7 %collective-permute-done = bf16[512,2048]{1,0:T(8,128)(2,1)S(1)} collective-permute-done((bf16[512,2048]{1,0:T(8,128)(2,1)}, bf16[512,2048]{1,0:T(8,128)(2,1)S(1)}, u32[]{:S(2)}, u32[]{:S(2)}) %collective-permute-start) | collective-permute-done | bytes 2097184 | tf_op jit(solution)/shard_map/ppermute | solution.py:12
  144.6 0.0 reduce-scatter.2.cloned.1.call-done
  144.6 1.3 copy.9
  (3 shorter events, 0.0 us)
Async XLA Ops:
  7.2 51.1 %all-gather.5.cloned.1.call-start = ((), (), s32[]{:S(2)}) async-start(), calls=%async_computation.2 | async-start | bytes 2621440 | tf_op jit(solution)/shard_map/all_gather | solution.py:27
  7.9 136.7 %reduce-scatter.2.cloned.1.call-start = ((), (), s32[]{:S(2)}) async-start(), calls=%async_computation.1 | async-start | bytes 10485760 | tf_op jit(solution)/shard_map/reduce_scatter | solution.py:45
  68.4 1.6 %copy-start = (bf16[1,1,512,2048]{3,2,1,0:T(8,128)(2,1)S(1)}, bf16[1,1,512,2048]{3,2,1,0:T(8,128)(2,1)}, u32[]{:S(2)}) copy-start(bf16[1,1,512,2048]{3,2,1,0:T(8,128)(2,1)} %param.5) | copy-start | bytes 6291460
  96.6 48.0 %collective-permute-start = (bf16[512,2048]{1,0:T(8,128)(2,1)}, bf16[512,2048]{1,0:T(8,128)(2,1)S(1)}, u32[]{:S(2)}, u32[]{:S(2)}) collective-permute-start(bf16[512,2048]{1,0:T(8,128)(2,1)} %fusion.10), channel_id=1, source_target_pairs={{4,0},{5,1},{6,2},{7,3},{12,8},{13,9},{14,10},{15,11},{20,16},{21,... | collective-permute-start | bytes 6291464 | tf_op jit(solution)/shard_map/ppermute | solution.py:12
Sparse Core Ops, SparseCore 0:
  9.6 48.6 all-gather.4
  68.5 70.9 reduce-scatter.1
